TPU v7x, 256 devices: a whole 4x4x8 slice. The times are simulated.
256 devices in a mesh: req: 32 (over y, x, core), tp: 8 (over z).
Axes of the slice: x: 4, y: 4, z: 8, core: 2. Of those that a mesh axis runs over, the one named last changes fastest.
Arguments:
- tokens: bfloat16 [256, 4, 1536], P('req'), may hold values from -6 to 6
- lengths: int32 [256], P('req'), may hold values from 16 to 32768, as said below
- page_table: int32 [256, 9], P('req'), may hold values from 0 to 2303, as said below
- kv_pages: bfloat16 [2304, 2, 128, 128], P('req'), may hold values from -480 to 480
- norm_gain: float32 [1536], replicated, may hold values from 0.1 to 1.9
- query_weight: bfloat16 [1536, 1024], P(None, 'tp'), may hold values from -0.15625 to 0.15625
- key_weight: bfloat16 [1536, 128], replicated, may hold values from -0.15625 to 0.15625
- value_weight: bfloat16 [1536, 128], replicated, may hold values from -0.15625 to 0.15625
- out_weight: bfloat16 [1024, 1536], P('tp'), may hold values from -0.1875 to 0.1875
- mlp_gain: float32 [1536], replicated, may hold values from 0.1 to 1.9
- gate_weight: bfloat16 [1536, 4608], P(None, 'tp'), may hold values from -0.15625 to 0.15625
- up_weight: bfloat16 [1536, 4608], P(None, 'tp'), may hold values from -0.15625 to 0.15625
- down_weight: bfloat16 [4608, 1536], P('tp'), may hold values from -0.09375 to 0.09375
Outputs:
- layer_out: bfloat16 [256, 4, 1536], P('req')
Inputs may be any that keep to these rules, and one draw needn't show every extreme that they name: `lengths`: one request has exactly 32768 cached positions in every draw. `page_table`: all entries together are a permutation of the 2304 pool pages. Entry (r, j) is pool page r * 9 + j, in the part of the pool held with request r, except for spilled entries chosen from the seed (about a fifth of all); the spilled entries hold one another's pool pages in an order drawn from the seed, mostly on other devices of req.
All inputs are finite; a program needn't handle non-finite values.
Results may differ from a plain program's by a relative error of at most 0.0095.
The roundings to bfloat16 on the way count: a program that leaves them out, or rounds other values in their place, can miss the bound.
Values may be sent and summed in bfloat16 or wider, within the bound.
No kernel may reach another device: no remote copies, remote signals or barrier semaphores. Data moves between devices by JAX's collectives and lax.ppermute only.
A program may use at most 128 MiB of HBM per device.

v0:
```python
import jax
import jax.numpy as jnp
from jax import lax
from jax.sharding import PartitionSpec as P

WINDOW = 1024
negative = -1e30
epsilon = 1e-06


def rms_norm(values, gain):
    return values * lax.rsqrt(jnp.mean(values * values, axis=-1, keepdims=True) + epsilon) * gain


def body(
    tokens,
    lengths,
    page_table,
    kv_pages,
    norm_gain,
    query_weight,
    key_weight,
    value_weight,
    out_weight,
    mlp_gain,
    gate_weight,
    up_weight,
    down_weight,
):
    req_dev, steps, width = tokens.shape
    head_dim = key_weight.shape[1]
    heads_dev = query_weight.shape[1] // head_dim
    pool_size = kv_pages.shape[0]
    page_size = kv_pages.shape[2]
    window_pages = page_table.shape[1]
    token_rows = tokens.reshape(req_dev * steps, width)
    normed = rms_norm(token_rows.astype(jnp.float32), norm_gain).astype(jnp.bfloat16)
    queries = (
        jnp.dot(normed, query_weight, preferred_element_type=jnp.float32) * head_dim ** (-0.5)
    ).astype(jnp.bfloat16)
    key_new = jnp.dot(normed, key_weight, preferred_element_type=jnp.float32).astype(jnp.bfloat16)
    value_new = jnp.dot(normed, value_weight, preferred_element_type=jnp.float32).astype(
        jnp.bfloat16
    )
    all_lengths, all_table = (
        lax.all_gather(lengths, "req", axis=0, tiled=True),
        lax.all_gather(page_table, "req", axis=0, tiled=True),
    )
    all_queries = lax.all_gather(
        queries.reshape(req_dev, steps, heads_dev * head_dim), "req", axis=0, tiled=True
    )
    requests = all_lengths.shape[0]
    flat_table = all_table.reshape(-1)
    local_slot = flat_table - lax.axis_index("req") * pool_size
    inside = (local_slot >= 0) & (local_slot < pool_size)
    owner_entry = (
        jnp.zeros((pool_size,), jnp.int32)
        .at[jnp.where(inside, local_slot, pool_size)]
        .set(jnp.arange(flat_table.shape[0], dtype=jnp.int32), mode="drop")
    )
    page_request = owner_entry // window_pages
    page_number = owner_entry % window_pages
    page_length = all_lengths[page_request]
    first_page = jnp.maximum(page_length - (WINDOW - 1), 0) // page_size
    position = (first_page + page_number)[:, None] * page_size + jnp.arange(
        page_size, dtype=jnp.int32
    )[None, :]
    current = page_length[:, None] + jnp.arange(steps, dtype=jnp.int32)[None, :]
    visible = (position[:, None, :] < page_length[:, None, None]) & (
        position[:, None, :] > current[:, :, None] - WINDOW
    )
    visible = visible[:, :, None, :]
    page_queries = all_queries[page_request]
    scores = jnp.einsum(
        "pqd,pkd->pqk", page_queries, kv_pages[:, 0], preferred_element_type=jnp.float32
    )
    scores = jnp.where(visible, scores.reshape(pool_size, steps, heads_dev, page_size), negative)
    block_max = jnp.max(scores, axis=-1)
    weights = jnp.where(visible, jnp.exp(scores - block_max[..., None]), 0.0)
    block_total = jnp.sum(weights, axis=-1)
    block_out = jnp.einsum(
        "pqk,pkd->pqd",
        weights.astype(jnp.bfloat16).reshape(pool_size, steps * heads_dev, page_size),
        kv_pages[:, 1],
        preferred_element_type=jnp.float32,
    )
    block_out = block_out.reshape(pool_size, steps, heads_dev, head_dim)
    request_max = jnp.maximum(
        jax.ops.segment_max(block_max, page_request, num_segments=requests), negative
    )
    start_row = lax.axis_index("req") * req_dev
    cache_max = lax.pmax(request_max, "req")
    scale = jnp.exp(block_max - cache_max[page_request])
    sent_out = jax.ops.segment_sum(
        block_out * scale[..., None], page_request, num_segments=requests
    )
    sent_total = jax.ops.segment_sum(block_total * scale, page_request, num_segments=requests)
    cache_out, cache_total = (
        lax.psum_scatter(sent_out, "req", scatter_dimension=0, tiled=True),
        lax.psum_scatter(sent_total, "req", scatter_dimension=0, tiled=True),
    )
    mine_max = lax.dynamic_slice_in_dim(cache_max, start_row, req_dev, 0)
    local_queries = queries.reshape(req_dev, steps, heads_dev, head_dim)
    new_scores = jnp.einsum(
        "rshd,rtd->rsht",
        local_queries,
        key_new.reshape(req_dev, steps, head_dim),
        preferred_element_type=jnp.float32,
    )
    causal = (jnp.arange(steps)[None, :] <= jnp.arange(steps)[:, None])[None, :, None, :]
    new_scores = jnp.where(causal, new_scores, negative)
    new_max = jnp.max(new_scores, axis=-1)
    new_weights = jnp.where(causal, jnp.exp(new_scores - new_max[..., None]), 0.0)
    new_total = jnp.sum(new_weights, axis=-1)
    new_out = jnp.einsum(
        "rsht,rtd->rshd",
        new_weights.astype(jnp.bfloat16),
        value_new.reshape(req_dev, steps, head_dim),
        preferred_element_type=jnp.float32,
    )
    overall = jnp.maximum(mine_max, new_max)
    cache_scale = jnp.exp(mine_max - overall)
    new_scale = jnp.exp(new_max - overall)
    total = cache_total * cache_scale + new_total * new_scale
    summed = cache_out * cache_scale[..., None] + new_out * new_scale[..., None]
    attended = (
        (summed / total[..., None])
        .astype(jnp.bfloat16)
        .reshape(req_dev * steps, heads_dev * head_dim)
    )
    projected = jnp.dot(attended, out_weight, preferred_element_type=jnp.float32)
    attn_total = lax.psum(projected, "tp")
    residual = (token_rows.astype(jnp.float32) + attn_total).astype(jnp.bfloat16)
    mlp_in = rms_norm(residual.astype(jnp.float32), mlp_gain).astype(jnp.bfloat16)
    gate = jnp.dot(mlp_in, gate_weight, preferred_element_type=jnp.float32)
    upward = jnp.dot(mlp_in, up_weight, preferred_element_type=jnp.float32)
    hidden = (jax.nn.gelu(gate, approximate=True) * upward).astype(jnp.bfloat16)
    mlp_total = lax.psum(
        jnp.dot(hidden, down_weight, preferred_element_type=jnp.float32).astype(jnp.bfloat16), "tp"
    ).astype(jnp.float32)
    layer_out = (residual.astype(jnp.float32) + mlp_total).astype(jnp.bfloat16)
    return layer_out.reshape(req_dev, steps, width)


def solution(mesh):
    return jax.shard_map(
        body,
        mesh=mesh,
        in_specs=(
            P("req", None, None),
            P("req"),
            P("req", None),
            P("req", None, None, None),
            P(),
            P(None, "tp"),
            P(),
            P(),
            P("tp", None),
            P(),
            P(None, "tp"),
            P(None, "tp"),
            P("tp", None),
        ),
        out_specs=P("req", None, None),
        check_vma=False,
    )
```

profile of v0, /device:TPU:2, one launch (start us, length us, event | category | flops | bytes accessed | tf_op | source)
XLA Modules:
  0.0 512.9 jit_solution(16299514413610461038)
XLA Ops:
  6.5 1.4 fusion.63
  8.6 0.9 dynamic-update-slice
  9.5 15.7 %all-reduce = s32[256]{0:T(256)S(1)} all-reduce(s32[256]{0:T(256)S(1)} %dynamic-update-slice), channel_id=1, replica_groups=mesh['req'=32,'tp'=8] {'req'}, use_global_device_ids=true, to_apply=%add | all-reduce | flops 256 | bytes 2048
  25.2 23.4 %all_gather.9 = s32[256,9]{1,0:T(8,128)S(1)} all-gather(s32[8,9]{1,0:T(8,128)} %param.15), channel_id=1, replica_groups=mesh['req'=32,'tp'=8] {'req'}, dimensions={0}, use_global_device_ids=true | all-gather | bytes 9504 | tf_op jit(solution)/shard_map/all_gather | solution.py:47
  48.5 0.2 sub.78
  48.8 9.0 %scatter_custom_fusion = s32[72]{0:T(128)S(1)} fusion(s32[2304]{0:T(1024)S(1)} %fusion.44, s32[2304]{0:T(1024)S(1)} %iota.34, s32[]{:T(128)} %constant.27.clone.1), kind=kCustom, calls=%fused_computation.93 | custom fusion | bytes 292 | tf_op jit(solution)/shard_map/scatter | solution.py:59
  57.8 1.3 gather_fusion
  59.4 1.0 multiply_reduce_fusion
  60.4 0.9 reshape.246
  61.4 0.8 multiply_convert_fusion
  62.4 22.6 %all_gather.11 = bf16[256,4,128]{2,1,0:T(4,128)(2,1)S(1)} all-gather(bf16[8,4,128]{2,1,0:T(4,128)(2,1)S(1)} %bitcast.89), channel_id=1, replica_groups=mesh['req'=32,'tp'=8] {'req'}, dimensions={0}, use_global_device_ids=true | all-gather | bytes 270336 | tf_op jit(solution)/shard_map/all_gather | solution.py:49
  85.0 0.7 gather_fusion.1
  85.7 3.1 fusion.64
  88.8 1.0 scatter_custom_fusion.1
  89.8 123.3 %pmax.7 = f32[256,4,1]{1,0,2:T(8,128)S(1)} all-reduce(f32[256,4,1]{1,0,2:T(8,128)S(1)} %maximum_bitcast_fusion), channel_id=1, replica_groups=mesh['req'=32,'tp'=8] {'req'}, use_global_device_ids=true, to_apply=%region_4.5 | all-reduce | flops 1024 | bytes 8192 | tf_op jit(solution)/shard_map/pmax | solution.py:92
  213.1 0.6 gather_fusion.2
  213.8 2.5 fusion.9
  216.3 3.5 scatter_fusion
  219.8 0.8 copy.86
  221.7 1.3 fusion.57
  222.9 1.2 scatter_custom_fusion.3
  224.7 123.8 %all-reduce.1 = f32[256,4,1]{1,0,2:T(8,128)S(1)} all-reduce(f32[256,4,1]{1,0,2:T(8,128)S(1)} %bitcast.88), channel_id=3, replica_groups=mesh['req'=32,'tp'=8] {'req'}, use_global_device_ids=true, to_apply=%region_10.11.clone | all-reduce | flops 1024 | bytes 8192
  348.6 1.2 convolution_convert_fusion.1
  349.8 0.7 reshape.332
  350.7 0.9 fusion.66
  351.6 75.7 %all-reduce.5.cloned.1.call-done = f32[32,1536]{1,0:T(8,128)} async-done(((f32[32,1536]{1,0:T(8,128)}), f32[32,1536]{1,0:T(8,128)}) %all-reduce.5.cloned.1.call-update) | async-done | bytes 196624 | tf_op jit(solution)/shard_map/psum | solution.py:132
  427.3 1.1 fusion.18
  428.4 2.1 fusion.42
  430.5 3.2 convolution_convert_fusion
  433.7 71.0 %all-reduce.7.cloned.1.call-done = bf16[32,1536]{1,0:T(8,128)(2,1)} async-done(((bf16[32,1536]{1,0:T(8,128)(2,1)}), bf16[32,1536]{1,0:T(8,128)(2,1)}) %all-reduce.7.cloned.1.call-update) | async-done | bytes 98320 | tf_op jit(solution)/shard_map/psum | solution.py:138
  504.8 0.9 fusion.21
  505.7 0.7 reshape.245
  (55 shorter events, 1.9 us)
Async XLA Ops:
  6.5 424.0 %copy-start = (bf16[576,1536]{1,0:T(8,128)(2,1)S(1)}, bf16[576,1536]{1,0:T(8,128)(2,1)}, u32[]{:S(2)}) copy-start(bf16[576,1536]{1,0:T(8,128)(2,1)} %param.25) | copy-start | bytes 5308420
  6.5 55.7 %copy-start.2 = (bf16[1536,128]{1,0:T(8,128)(2,1)S(1)}, bf16[1536,128]{1,0:T(8,128)(2,1)}, u32[]{:S(2)}) copy-start(bf16[1536,128]{1,0:T(8,128)(2,1)} %param.18) | copy-start | bytes 1179652
  6.5 343.3 %reduce-scatter.6.cloned.1.call-start = ((), (), s32[]{:S(2)}) async-start(), calls=%async_computation.3 | async-start | bytes 540672
  59.2 154.5 %copy-start.8 = (pred[72,128]{1,0:T(8,128)(4,1)}, pred[72,128]{1,0:T(8,128)(4,1)S(1)}, u32[]{:S(2)}) copy-start(pred[72,128]{1,0:T(8,128)(4,1)S(1)} %broadcast_compare_fusion) | copy-start | bytes 27652
  59.3 154.5 %copy-start.4 = (s32[72,128]{1,0:T(8,128)}, s32[72,128]{1,0:T(8,128)S(1)}, u32[]{:S(2)}) copy-start(s32[72,128]{1,0:T(8,128)S(1)} %iota_add_fusion) | copy-start | bytes 110596
  59.4 154.4 %copy-start.5 = (s32[72,4]{1,0:T(8,128)}, s32[72,4]{1,0:T(8,128)S(1)}, u32[]{:S(2)}) copy-start(s32[72,4]{1,0:T(8,128)S(1)} %add_add_fusion) | copy-start | bytes 3460
  88.8 125.0 %copy-start.7 = (f32[72,4,128]{2,1,0:T(4,128)}, f32[72,4,128]{2,1,0:T(4,128)S(1)}, u32[]{:S(2)}) copy-start(f32[72,4,128]{2,1,0:T(4,128)S(1)} %get-tuple-element.17) | copy-start | bytes 442372
  213.7 2.6 copy-start.6
  216.3 4.5 copy-start.3
  219.8 130.8 %copy-start.1 = (bf16[128,1536]{1,0:T(8,128)(2,1)S(1)}, bf16[128,1536]{1,0:T(8,128)(2,1)}, u32[]{:S(2)}) copy-start(bf16[128,1536]{1,0:T(8,128)(2,1)} %param.21) | copy-start | bytes 1179652
  220.7 207.7 %copy-start.9 = (f32[1536]{0:T(1024)S(1)}, f32[1536]{0:T(1024)}, u32[]{:S(2)}) copy-start(f32[1536]{0:T(1024)} %param.22) | copy-start | bytes 18436
  220.7 206.6 %all-reduce.5.cloned.1.call-start = ((), (), s32[]{:S(2)}) async-start(), calls=%async_computation.1 | async-start | bytes 393216 | tf_op jit(solution)/shard_map/psum | solution.py:132
  351.6 153.2 %all-reduce.7.cloned.1.call-start = ((), (), s32[]{:S(2)}) async-start(), calls=%async_computation.2 | async-start | bytes 196608 | tf_op jit(solution)/shard_map/psum | solution.py:138
Sparse Core Ops, SparseCore 0:
  220.8 87.7 reduce-scatter.5
  351.7 75.5 all-reduce.4
  433.8 70.8 all-reduce.6
where the time goes:
time: 514 us; the launch traced here: 513 us
  blocking collectives  309 us (60%)
  waiting for transfers between devices  147 us (29%)
  local copies, waits for them, and re-layouts  17.7 us (3%)
  between operations  14.6 us (3%)
  matrix products  13.5 us (3%)
  other arithmetic  11.4 us (2%)
    unnamed x2, blocking collectives  140 us
    pmax x1, blocking collectives, body(): cache_max = lax.pmax(request_max, 'req')  123 us
    psum x1, waiting for transfers between devices, body(): attn_total = lax.psum(projected, 'tp')  75.7 us
    psum x1, waiting for transfers between devices, body(): lax.psum(jnp.dot(hidden, down_weight, preferred_element_type=jnp.float32)...  71 us
    all_gather x1, blocking collectives, body(): lax.all_gather(page_table, 'req', axis=0, tiled=True)  23.4 us
    all_gather x1, blocking collectives, body(): lax.all_gather(queries.reshape(req_dev, steps, heads_dev * head_dim), 're...  22.6 us
  transfers between devices with their start and end apart: 3, of which 2 were waited for; matrix products, arithmetic and copies ran while one was open for 1% of the time, Pallas kernels for 0%

commit v1 on v0

--- a/solution.py
+++ b/solution.py
@@ -6,6 +6,11 @@
 WINDOW = 1024
 negative = -1e30
 epsilon = 1e-06
+
+
+def fill_members_all_all(mine_x, comm_axis):
+    raw_out = lax.all_gather(mine_x, comm_axis).sum(axis=0)
+    return raw_out
 
 
 def rms_norm(values, gain):
@@ -135,7 +140,7 @@
     gate = jnp.dot(mlp_in, gate_weight, preferred_element_type=jnp.float32)
     upward = jnp.dot(mlp_in, up_weight, preferred_element_type=jnp.float32)
     hidden = (jax.nn.gelu(gate, approximate=True) * upward).astype(jnp.bfloat16)
-    mlp_total = lax.psum(
+    mlp_total = fill_members_all_all(
         jnp.dot(hidden, down_weight, preferred_element_type=jnp.float32).astype(jnp.bfloat16), "tp"
     ).astype(jnp.float32)
     layer_out = (residual.astype(jnp.float32) + mlp_total).astype(jnp.bfloat16)

time: 514 us -> 469 us (0.912)
  waiting for transfers between devices: 147 us -> 75.9 us
  blocking collectives: 309 us -> 335 us
    psum x1 -> x0, waiting for transfers between devices: 71 us -> none  [body(): lax.psum(jnp.dot(hidden, down_weight, preferred_element_type=jnp.float32)...]
    all_gather x0 -> x1, blocking collectives: none -> 26.5 us  [fill_members_all_all(): raw_out = lax.all_gather(mine_x, comm_axis).sum(axis=0)]
  transfers between devices with their start and end apart: 3 -> 2, of which waited for: 2 -> 1; matrix products, arithmetic and copies ran while one was open for 1% -> 1% of each run, Pallas kernels for 0% -> 0%
where the time goes in v1:
time: 469 us
  blocking collectives  335 us (71%)
  waiting for transfers between devices  75.9 us (16%)
  local copies, waits for them, and re-layouts  18.3 us (4%)
  between operations  15 us (3%)
  matrix products  13.6 us (3%)
  other arithmetic  10.6 us (2%)
    unnamed x2, blocking collectives  139 us
    pmax x1, blocking collectives, body(): cache_max = lax.pmax(request_max, 'req')  123 us
    psum x1, waiting for transfers between devices, body(): attn_total = lax.psum(projected, 'tp')  75.8 us
    all_gather x1, blocking collectives, fill_members_all_all(): raw_out = lax.all_gather(mine_x, comm_axis).sum(axis=0)  26.5 us
    all_gather x1, blocking collectives, body(): lax.all_gather(page_table, 'req', axis=0, tiled=True)  23.4 us
    all_gather x1, blocking collectives, body(): lax.all_gather(queries.reshape(req_dev, steps, heads_dev * head_dim), 're...  22.6 us
  transfers between devices with their start and end apart: 2, of which 1 were waited for; matrix products, arithmetic and copies ran while one was open for 1% of the time, Pallas kernels for 0%

profile of v1, /device:TPU:2, one launch (start us, length us, event | category | flops | bytes accessed | tf_op | source)
XLA Modules:
  0.0 468.6 jit_solution(1292504064180353443)
XLA Ops:
  6.5 1.4 fusion.63
  8.6 0.9 dynamic-update-slice
  9.5 15.7 %all-reduce = s32[256]{0:T(256)S(1)} all-reduce(s32[256]{0:T(256)S(1)} %dynamic-update-slice), channel_id=1, replica_groups=mesh['req'=32,'tp'=8] {'req'}, use_global_device_ids=true, to_apply=%add | all-reduce | flops 256 | bytes 2048
  25.2 23.4 %all_gather.15 = s32[256,9]{1,0:T(8,128)S(1)} all-gather(s32[8,9]{1,0:T(8,128)} %param.15), channel_id=1, replica_groups=mesh['req'=32,'tp'=8] {'req'}, dimensions={0}, use_global_device_ids=true | all-gather | bytes 9504 | tf_op jit(solution)/shard_map/all_gather | solution.py:52
  48.5 0.2 sub.78
  48.8 9.0 %scatter_custom_fusion = s32[72]{0:T(128)S(1)} fusion(s32[2304]{0:T(1024)S(1)} %fusion.44, s32[2304]{0:T(1024)S(1)} %iota.34, s32[]{:T(128)} %constant.28.clone.1), kind=kCustom, calls=%fused_computation.93 | custom fusion | bytes 292 | tf_op jit(solution)/shard_map/scatter | solution.py:64
  57.8 1.3 gather_fusion
  59.4 1.0 multiply_reduce_fusion
  60.4 0.9 reshape.246
  61.4 0.8 multiply_convert_fusion
  62.4 22.6 %all_gather.17 = bf16[256,4,128]{2,1,0:T(4,128)(2,1)S(1)} all-gather(bf16[8,4,128]{2,1,0:T(4,128)(2,1)S(1)} %bitcast.91), channel_id=1, replica_groups=mesh['req'=32,'tp'=8] {'req'}, dimensions={0}, use_global_device_ids=true | all-gather | bytes 270336 | tf_op jit(solution)/shard_map/all_gather | solution.py:54
  85.0 0.7 gather_fusion.1
  85.7 3.1 fusion.64
  88.8 1.0 scatter_custom_fusion.1
  89.8 123.3 %pmax.7 = f32[256,4,1]{1,0,2:T(8,128)S(1)} all-reduce(f32[256,4,1]{1,0,2:T(8,128)S(1)} %maximum_bitcast_fusion), channel_id=1, replica_groups=mesh['req'=32,'tp'=8] {'req'}, use_global_device_ids=true, to_apply=%region_4.5 | all-reduce | flops 1024 | bytes 8192 | tf_op jit(solution)/shard_map/pmax | solution.py:97
  213.1 0.6 gather_fusion.2
  213.8 2.5 fusion.9
  216.3 3.5 scatter_fusion
  219.8 0.8 copy.86
  221.7 1.3 fusion.57
  222.9 1.2 scatter_custom_fusion.3
  224.7 123.8 %all-reduce.1 = f32[256,4,1]{1,0,2:T(8,128)S(1)} all-reduce(f32[256,4,1]{1,0,2:T(8,128)S(1)} %bitcast.90), channel_id=4, replica_groups=mesh['req'=32,'tp'=8] {'req'}, use_global_device_ids=true, to_apply=%region_10.11.clone | all-reduce | flops 1024 | bytes 8192
  348.6 1.2 convolution_convert_fusion.1
  349.8 0.7 reshape.333
  350.7 0.9 fusion.66
  351.6 75.8 %all-reduce.4.cloned.1.call-done = f32[32,1536]{1,0:T(8,128)} async-done(((f32[32,1536]{1,0:T(8,128)}), f32[32,1536]{1,0:T(8,128)}) %all-reduce.4.cloned.1.call-update) | async-done | bytes 196624 | tf_op jit(solution)/shard_map/psum | solution.py:137
  427.4 1.1 fusion.18
  428.5 0.6 copy-done.2
  429.1 2.8 fusion.42
  431.9 2.6 convolution_convert_fusion
  434.5 26.5 %all-gather = bf16[256,1536]{1,0:T(8,128)(2,1)S(1)} all-gather(bf16[32,1536]{1,0:T(8,128)(2,1)} %convolution_convert_fusion), channel_id=2, replica_groups=mesh['req'=32,'tp'=8] {'tp'}, dimensions={0}, use_global_device_ids=true | all-gather | bytes 884736 | tf_op jit(solution)/shard_map/all_gather | solution.py:12
  461.1 0.7 reshape.245
  (60 shorter events, 2.0 us)
Async XLA Ops:
  6.5 425.3 %copy-start = (bf16[576,1536]{1,0:T(8,128)(2,1)S(1)}, bf16[576,1536]{1,0:T(8,128)(2,1)}, u32[]{:S(2)}) copy-start(bf16[576,1536]{1,0:T(8,128)(2,1)} %param.25) | copy-start | bytes 5308420
  6.5 55.7 %copy-start.5 = (bf16[1536,128]{1,0:T(8,128)(2,1)S(1)}, bf16[1536,128]{1,0:T(8,128)(2,1)}, u32[]{:S(2)}) copy-start(bf16[1536,128]{1,0:T(8,128)(2,1)} %param.18) | copy-start | bytes 1179652
  6.5 343.3 %reduce-scatter.6.cloned.1.call-start = ((), (), s32[]{:S(2)}) async-start(), calls=%async_computation.2 | async-start | bytes 540672
  59.2 154.5 %copy-start.11 = (pred[72,128]{1,0:T(8,128)(4,1)}, pred[72,128]{1,0:T(8,128)(4,1)S(1)}, u32[]{:S(2)}) copy-start(pred[72,128]{1,0:T(8,128)(4,1)S(1)} %broadcast_compare_fusion) | copy-start | bytes 27652
  59.3 154.5 %copy-start.7 = (s32[72,128]{1,0:T(8,128)}, s32[72,128]{1,0:T(8,128)S(1)}, u32[]{:S(2)}) copy-start(s32[72,128]{1,0:T(8,128)S(1)} %iota_add_fusion) | copy-start | bytes 110596
  59.4 154.4 %copy-start.8 = (s32[72,4]{1,0:T(8,128)}, s32[72,4]{1,0:T(8,128)S(1)}, u32[]{:S(2)}) copy-start(s32[72,4]{1,0:T(8,128)S(1)} %add_add_fusion) | copy-start | bytes 3460
  88.8 125.0 %copy-start.10 = (f32[72,4,128]{2,1,0:T(4,128)}, f32[72,4,128]{2,1,0:T(4,128)S(1)}, u32[]{:S(2)}) copy-start(f32[72,4,128]{2,1,0:T(4,128)S(1)} %get-tuple-element.17) | copy-start | bytes 442372
  213.7 2.6 copy-start.9
  216.3 4.5 copy-start.6
  219.8 130.8 %copy-start.4 = (bf16[128,1536]{1,0:T(8,128)(2,1)S(1)}, bf16[128,1536]{1,0:T(8,128)(2,1)}, u32[]{:S(2)}) copy-start(bf16[128,1536]{1,0:T(8,128)(2,1)} %param.21) | copy-start | bytes 1179652
  220.7 206.7 %all-reduce.4.cloned.1.call-start = ((), (), s32[]{:S(2)}) async-start(), calls=%async_computation.1 | async-start | bytes 393216 | tf_op jit(solution)/shard_map/psum | solution.py:137
  349.8 82.1 %copy-start.12 = (f32[1536]{0:T(1024)S(1)}, f32[1536]{0:T(1024)}, u32[]{:S(2)}) copy-start(f32[1536]{0:T(1024)} %param.22) | copy-start | bytes 18436
  428.4 0.6 copy-start.2
  428.5 3.4 copy-start.1
  434.5 26.6 %copy-start.3 = (bf16[32,1536]{1,0:T(8,128)(2,1)S(1)}, bf16[32,1536]{1,0:T(8,128)(2,1)}, u32[]{:S(2)}) copy-start(bf16[32,1536]{1,0:T(8,128)(2,1)} %copy-done.2) | copy-start | bytes 294916
Sparse Core Ops, SparseCore 0:
  220.8 87.7 reduce-scatter.5
  351.7 75.6 all-reduce.3
